TPU v7x, 256 devices: a whole 4x4x8 slice. The times are simulated.
256 devices in a mesh: dp: 32 (over z, y), expert: 8 (over x, core).
Axes of the slice: x: 4, y: 4, z: 8, core: 2. Of those that a mesh axis runs over, the one named last changes fastest.
Arguments:
- residual: bfloat16 [2048, 4096], P(('dp', 'expert')), may hold values from -8.2 to 8.2
- queries: bfloat16 [2048, 4096], P('dp', 'expert'), may hold values from -24 to 24
- new_keys: bfloat16 [2048, 1024], P('dp', 'expert'), may hold values from -6 to 6
- new_values: bfloat16 [2048, 1024], P('dp', 'expert'), may hold values from -6 to 6
- cache_keys: bfloat16 [64, 1024, 1024], P('dp', None, 'expert'), may hold values from -8 to 8
- cache_values: bfloat16 [64, 1024, 1024], P('dp', None, 'expert'), may hold values from -6 to 6
- out_weight: bfloat16 [4096, 4096], P('expert', 'dp'), may hold values from -1 to 1
- ffn_gain: float32 [4096], replicated, may hold values from 0.1 to 1.9
- router: bfloat16 [4096, 8], replicated, may hold values from -0.0234375 to 0.0234375
- routes: int32 [2048, 2], P(('dp', 'expert')), may hold values from 0 to 7, all different within a row; in each aligned block of 64 rows (0 to 63, 64 to 127, ...) at most 24 rows name the same one
- w_gate: bfloat16 [8, 4096, 14336], P('expert', None, 'dp'), may hold values from -0.09375 to 0.09375
- w_up: bfloat16 [8, 4096, 14336], P('expert', None, 'dp'), may hold values from -0.09375 to 0.09375
- w_down: bfloat16 [8, 14336, 4096], P('expert', 'dp'), may hold values from -0.046875 to 0.046875
- summary_gain: float32 [4096], P('expert'), may hold values from 0.1 to 1.9
- reduce_scale: float32 [32], P('expert'), may hold values from 0.1 to 30
- assign: int32 [64], replicated, may hold values from 0 to 3
Outputs:
- summary: bfloat16 [64, 4096], P('dp', 'expert')
- reduced: bfloat16 [64, 4096], P('dp', 'expert')
Inputs may be any that keep to these rules, and one draw needn't show every extreme that they name: `routes`: each token names 2 different experts and every expert is named by some token; among the tokens of one dp index (aligned blocks of 64 rows) no expert is named by more than 24 tokens, and that bound is reached in some block.
All inputs are finite; a program needn't handle non-finite values.
Results may differ from a plain program's by a relative error of at most 0.017.
Values may be sent and summed in bfloat16 or wider, within the bound.
No kernel may reach another device: no remote copies, remote signals or barrier semaphores. Data moves between devices by JAX's collectives and lax.ppermute only.
A program may use at most 128 MiB of HBM per device.

v0:
```python
import math
import jax
import jax.numpy as jnp
from jax import lax
from jax.sharding import PartitionSpec as P

HEADS = 32
KVH = 8
HD = 128
EXPERTS = 8
WIN = 32
GROUP_CAP = 24
EPSILON = 1e-05


def attend(queries, new_keys, new_values, cache_keys, cache_values):
    span_count, cache_len, kv_width = cache_keys.shape
    kv_local = kv_width // HD
    group = HEADS // KVH
    window = queries.shape[0] // span_count
    query_view = queries.reshape(span_count, window, kv_local, group, HD)
    fresh_keys = new_keys.reshape(span_count, window, kv_local, HD)
    fresh_values = new_values.reshape(span_count, window, kv_local, HD)
    stored_keys = cache_keys.reshape(span_count, cache_len, kv_local, HD)
    stored_values = cache_values.reshape(span_count, cache_len, kv_local, HD)
    factor = 1.0 / math.sqrt(HD)
    past_scores = (
        jnp.einsum("ctkgd,cpkd->ckgtp", query_view, stored_keys, preferred_element_type=jnp.float32)
        * factor
    )
    fresh_scores = (
        jnp.einsum("ctkgd,cskd->ckgts", query_view, fresh_keys, preferred_element_type=jnp.float32)
        * factor
    )
    causal = jnp.arange(window)[:, None] >= jnp.arange(window)[None, :]
    fresh_scores = jnp.where(causal, fresh_scores, -jnp.inf)
    highest = jnp.maximum(jnp.max(past_scores, axis=-1), jnp.max(fresh_scores, axis=-1))[..., None]
    past_exp = jnp.exp(past_scores - highest)
    fresh_exp = jnp.exp(fresh_scores - highest)
    totals = jnp.sum(past_exp, axis=-1, keepdims=True) + jnp.sum(fresh_exp, axis=-1, keepdims=True)
    past_weights = (past_exp / totals).astype(jnp.bfloat16)
    fresh_weights = (fresh_exp / totals).astype(jnp.bfloat16)
    context = jnp.einsum(
        "ckgtp,cpkd->ctkgd", past_weights, stored_values, preferred_element_type=jnp.float32
    )
    context = context + jnp.einsum(
        "ckgts,cskd->ctkgd", fresh_weights, fresh_values, preferred_element_type=jnp.float32
    )
    return context.astype(jnp.bfloat16).reshape(span_count * window, kv_local * group * HD)


def shards(
    residual,
    queries,
    new_keys,
    new_values,
    cache_keys,
    cache_values,
    out_weight,
    ffn_gain,
    router,
    routes,
    w_gate,
    w_up,
    w_down,
    summary_gain,
    reduce_scale,
    assign,
):
    expert_count = lax.axis_size("expert")
    dp_index = lax.axis_index("dp")
    column = lax.axis_index("expert")
    span_local = cache_keys.shape[0]
    tok_local = residual.shape[0]
    width = residual.shape[1]
    slice_width = width // expert_count
    highest_precision = lax.Precision.HIGHEST
    attended = attend(queries, new_keys, new_values, cache_keys, cache_values)
    head_terms = jnp.dot(
        attended,
        lax.all_gather(out_weight, "dp", axis=1, tiled=True),
        preferred_element_type=jnp.float32,
    )
    mixed = residual.astype(jnp.float32) + lax.psum_scatter(
        head_terms, "expert", scatter_dimension=0, tiled=True
    )
    normed = (
        mixed * lax.rsqrt(jnp.mean(mixed * mixed, axis=-1, keepdims=True) + EPSILON) * ffn_gain
    ).astype(jnp.bfloat16)
    expert_ids = jnp.arange(EXPERTS, dtype=jnp.int32)
    first = routes[:, 0:1] == expert_ids[None, :]
    second = routes[:, 1:2] == expert_ids[None, :]
    partner = jnp.where(first, routes[:, 1:2], jnp.where(second, routes[:, 0:1], -1))
    outgoing = jnp.where((partner >= 0).T[:, :, None], normed[None, :, :], 0)
    arrived_rows, arrived_partner = (
        lax.all_to_all(outgoing, "expert", split_axis=0, concat_axis=1, tiled=True),
        lax.all_to_all(partner.T, "expert", split_axis=0, concat_axis=1, tiled=True),
    )
    present = (arrived_partner >= 0).astype(jnp.int32)
    position = jnp.cumsum(present, axis=1) - 1
    picker = (present[:, None, :] > 0) & (
        position[:, None, :] == jnp.arange(GROUP_CAP)[None, :, None]
    )
    compact = jnp.einsum(
        "eks,esd->ked",
        picker.astype(jnp.bfloat16),
        arrived_rows,
        preferred_element_type=jnp.float32,
    ).astype(jnp.bfloat16)
    arrived_count = arrived_partner.shape[1]
    pick = picker[0]
    slot_present = jnp.any(pick, axis=1)
    slot_partner = jnp.sum(jnp.where(pick, arrived_partner[0][None, :], 0), axis=1)
    local_span = jnp.arange(arrived_count) // WIN
    slot_span = jnp.sum(jnp.where(pick, local_span[None, :], 0), axis=1)
    slot_logits = jnp.dot(compact[:, 0, :], router, preferred_element_type=jnp.float32)
    own_logit = jnp.sum(jnp.where(expert_ids[None, :] == column, slot_logits, 0.0), axis=-1)
    partner_logit = jnp.sum(
        jnp.where(expert_ids[None, :] == slot_partner[:, None], slot_logits, 0.0), axis=-1
    )
    slot_gate = jnp.where(slot_present, jax.nn.sigmoid(own_logit - partner_logit), 0.0)
    pool_weight = jnp.where(
        slot_span[:, None] == jnp.arange(span_local)[None, :], slot_gate[:, None], 0.0
    )
    gathered = lax.all_gather(compact, "dp", axis=0, tiled=True)
    gathered_weight = lax.all_gather(pool_weight, "dp", axis=0, tiled=True)
    n_dp = gathered.shape[0] // GROUP_CAP
    gate_proj = jnp.einsum("ned,edf->nf", gathered, w_gate, preferred_element_type=jnp.float32)
    up_proj = jnp.einsum("ned,edf->nf", gathered, w_up, preferred_element_type=jnp.float32)
    hidden = (jax.nn.silu(gate_proj) * up_proj).astype(jnp.bfloat16)
    span_hidden = jnp.einsum(
        "iks,ikf->isf",
        gathered_weight.reshape(n_dp, GROUP_CAP, span_local),
        hidden.reshape(n_dp, GROUP_CAP, -1).astype(jnp.float32),
        precision=highest_precision,
    ).reshape(n_dp * span_local, -1)
    pooled_part = jnp.dot(span_hidden, w_down[0].astype(jnp.float32), precision=highest_precision)
    own_span = dp_index * span_local + column * tok_local // WIN
    span_count = n_dp * span_local
    mixed_sum = jnp.sum(mixed, axis=0)
    pooled_part = pooled_part + jnp.where(
        (jnp.arange(span_count) == own_span)[:, None], mixed_sum[None, :], 0.0
    )
    pooled_cols = lax.psum_scatter(pooled_part, "expert", scatter_dimension=1, tiled=True)
    pooled_cols = lax.psum(pooled_cols, "dp")
    squares = lax.psum(jnp.sum(pooled_cols * pooled_cols, axis=-1), "expert")
    everyone = (pooled_cols * lax.rsqrt(squares / width + EPSILON)[:, None] * summary_gain).astype(
        jnp.bfloat16
    )
    summary = lax.dynamic_slice_in_dim(everyone, dp_index * span_local, span_local)
    heads_local = slice_width // HD
    mine = summary.reshape(span_local, heads_local, HD)
    others = everyone.reshape(everyone.shape[0], heads_local, HD)
    factor = reduce_scale / math.sqrt(HD)
    scores = (
        jnp.einsum("chd,khd->hck", mine, others, preferred_element_type=jnp.float32)
        * factor[:, None, None]
    )
    own_assign = lax.dynamic_slice_in_dim(assign, dp_index * span_local, span_local)
    same = own_assign[:, None] == assign[None, :]
    scores = jnp.where(same[None], scores, -jnp.inf)
    highest = jnp.max(scores, axis=-1, keepdims=True)
    expo = jnp.exp(scores - highest)
    weights = (expo / jnp.sum(expo, axis=-1, keepdims=True)).astype(jnp.bfloat16)
    reduced = jnp.einsum("hck,khd->chd", weights, others, preferred_element_type=jnp.float32)
    reduced = reduced.reshape(span_local, slice_width).astype(jnp.bfloat16)
    return (summary, reduced)


def solution(mesh):
    return jax.shard_map(
        shards,
        mesh=mesh,
        in_specs=(
            P(("dp", "expert"), None),
            P("dp", "expert"),
            P("dp", "expert"),
            P("dp", "expert"),
            P("dp", None, "expert"),
            P("dp", None, "expert"),
            P("expert", "dp"),
            P(),
            P(),
            P(("dp", "expert"), None),
            P("expert", None, "dp"),
            P("expert", None, "dp"),
            P("expert", "dp", None),
            P("expert"),
            P("expert"),
            P(),
        ),
        out_specs=(P("dp", "expert"), P("dp", "expert")),
        check_vma=False,
    )
```

profile of v0, /device:TPU:1, one launch (start us, length us, event | category | flops | bytes accessed | tf_op | source)
XLA Modules:
  0.0 459.1 jit_solution(10144320645197838944)
XLA Ops:
  7.2 0.0 copy-start
  7.2 0.0 all-gather.4.cloned.1.call-start
  7.2 0.7 all-gather.4.cloned.1.call-update
  7.9 0.0 reduce-scatter.3.cloned.1.call-start
  8.0 0.9 reshape.501
  8.9 0.4 fusion.59
  9.2 1.0 fusion.60
  10.3 0.3 fusion.27
  10.6 0.9 fusion.40
  11.5 0.0 copy-done.8
  11.5 0.4 fusion.22
  11.9 0.0 copy-start.5
  11.9 0.0 copy-start.1
  11.9 0.0 copy-start.2
  12.0 82.2 %all-gather.4.cloned.1.call-done = bf16[512,4096]{1,0:T(8,128)(2,1)} async-done(((bf16[512,128]{1,0:T(8,128)(2,1)}), bf16[512,4096]{1,0:T(8,128)(2,1)}) %all-gather.4.cloned.1.call-update) | async-done | bytes 4194320 | tf_op jit(solution)/shard_map/all_gather | solution.py:81
  94.2 4.0 fusion.35
  98.3 0.0 reduce-scatter.3.cloned.1.call-update
  98.3 0.6 compare_select_fusion.1
  98.9 7.7 %all-to-all-start = ((s32[8,1,8]{2,1,0:T(1,128)}), s32[8,1,8]{2,1,0:T(1,128)S(1)}, u32[]{:S(2)}, u32[]{:S(2)}) async-start(s32[8,1,8]{2,1,0:T(1,128)} %compare_select_fusion.1), calls=%async_computation | async-start | bytes 8192 | tf_op jit(solution)/shard_map/all_to_all | solution.py:97
  106.6 27.6 %reduce-scatter.3.cloned.1.call-done = f32[8,4096]{1,0:T(8,128)} async-done(((f32[64,4096]{1,0:T(8,128)}), f32[8,4096]{1,0:T(8,128)}) %reduce-scatter.3.cloned.1.call-update) | async-done | bytes 131088 | tf_op jit(solution)/shard_map/reduce_scatter | solution.py:84
  134.2 0.0 copy-done.1
  134.2 1.1 fusion.47
  135.3 1.0 multiply_convert_fusion.1
  136.3 0.9 broadcast_select_fusion
  137.2 0.0 all-to-all-done
  137.2 6.3 %all-to-all-start.1 = ((bf16[8,8,4096]{2,1,0:T(8,128)(2,1)}), bf16[8,8,4096]{2,1,0:T(8,128)(2,1)S(1)}, u32[]{:S(2)}, u32[]{:S(2)}) async-start(bf16[8,8,4096]{2,1,0:T(8,128)(2,1)} %broadcast_select_fusion), calls=%async_computation.2 | async-start | bytes 1048576 | tf_op jit(solution)/shard_map/all_to_all | solution.py:96
  143.5 0.5 broadcast.319
  144.0 0.7 fusion.58
  144.7 0.1 reshape.524
  144.8 0.1 reduce-window.7
  144.9 0.1 all_to_all.8
  145.0 0.1 add_reduce_fusion
  145.1 7.8 %all-to-all-done.1 = bf16[8,8,4096]{2,1,0:T(8,128)(2,1)S(1)} async-done(((bf16[8,8,4096]{2,1,0:T(8,128)(2,1)}), bf16[8,8,4096]{2,1,0:T(8,128)(2,1)S(1)}, u32[]{:S(2)}, u32[]{:S(2)}) %all-to-all-start.1) | async-done | bytes 524320 | tf_op jit(solution)/shard_map/all_to_all | solution.py:96
  152.9 0.9 convolution_convert_fusion
  153.8 0.0 all-gather.6.cloned.1.call-update
  153.8 0.0 reduce-scatter.5.cloned.1.call-start
  153.9 0.1 fusion.50
  154.0 0.1 select_reduce_fusion.1
  154.2 1.1 select_reduce_fusion.2
  155.3 36.3 %all-gather = f32[32,24,2]{1,2,0:T(2,128)S(1)} all-gather(f32[1,24,2]{1,2,0:T(2,128)S(1)} %fusion.56), channel_id=1, replica_groups=mesh['dp'=32,'expert'=8] {'dp'}, dimensions={0}, use_global_device_ids=true | all-gather | bytes 6336 | tf_op jit(solution)/shard_map/all_gather | solution.py:126
  191.6 49.7 %all-gather.6.cloned.1.call-done = bf16[768,1,4096]{2,0,1:T(8,128)(2,1)} async-done(((bf16[24,1,4096]{2,0,1:T(8,128)(2,1)}), bf16[768,1,4096]{2,0,1:T(8,128)(2,1)}) %all-gather.6.cloned.1.call-update) | async-done | bytes 6291472 | tf_op jit(solution)/shard_map/all_gather | solution.py:125
  241.3 7.0 %fusion.3 = f32[768,448]{0,1:T(8,128)S(1)} fusion(bf16[768,1,4096]{2,0,1:T(8,128)(2,1)} %all-gather.6.cloned.1.call-done, bf16[1,4096,448]{1,2,0:T(8,128)(2,1)} %param.26), kind=kOutput, calls=%fused_computation.3 | convolution fusion | flops 2818572288 | bytes 11337728 | tf_op jit(solution)/shard_map/ned,edf->nf/dot_general | solution.py:128
  248.3 0.0 copy-done.6
  248.4 3.1 fusion.14
  251.5 0.3 copy.46
  251.8 0.0 copy-start.10
  251.8 0.0 copy-start.11
  251.8 0.0 copy-start.3
  251.8 0.5 fusion.66
  252.3 0.1 reshape.513
  252.4 5.1 %convolution_add_fusion = f32[64,4096]{1,0:T(8,128)} fusion(f32[64,448]{1,0:T(8,128)S(1)} %reshape.513, bf16[1,448,4096]{2,1,0:T(8,128)(2,1)} %param.28, f32[4096]{0:T(1024)S(1)} %get-tuple-element.2, pred[64]{0:T(512)(128)(4,1)S(1)} %iota_compare_fusion.5), kind=kOutput, calls=%fused_computation.5 | convolution fusion | flops 1409810432 | bytes 4849728 | tf_op jit(solution)/shard_map/dot_general | solution.py:137
  257.5 0.0 reduce-scatter.5.cloned.1.call-update
  257.5 0.0 all-reduce.2.cloned.1.call-start
  257.6 0.1 dynamic_slice.7
  257.7 0.1 broadcast_compare_fusion
  257.8 30.3 %reduce-scatter.5.cloned.1.call-done = f32[64,512]{1,0:T(8,128)} async-done(((f32[64,4096]{1,0:T(8,128)}), f32[64,512]{1,0:T(8,128)}) %reduce-scatter.5.cloned.1.call-update) | async-done | bytes 131088 | tf_op jit(solution)/shard_map/reduce_scatter | solution.py:144
  288.0 0.0 all-reduce.2.cloned.1.call-update
  288.1 142.7 %all-reduce.2.cloned.1.call-done = f32[64,512]{1,0:T(8,128)} async-done(((f32[64,512]{1,0:T(8,128)}), f32[64,512]{1,0:T(8,128)}) %all-reduce.2.cloned.1.call-update) | async-done | bytes 131088 | tf_op jit(solution)/shard_map/psum | solution.py:145
  430.8 1.0 multiply_reduce_fusion
  431.8 16.7 %psum.15 = f32[64]{0:T(128)S(1)} all-reduce(f32[64]{0:T(128)S(1)} %multiply_reduce_fusion), channel_id=1, replica_groups=mesh['dp'=32,'expert'=8] {'expert'}, use_global_device_ids=true, to_apply=%region_16.17 | all-reduce | flops 64 | bytes 512 | tf_op jit(solution)/shard_map/psum | solution.py:146
  448.6 1.0 multiply_convert_fusion
  449.6 0.0 copy-start.4
  449.6 1.3 fusion.61
  450.9 1.7 fusion.26
  (31 shorter events, 0.2 us)
Async XLA Ops:
  7.2 1.7 copy-start
  7.2 4.3 copy-start.8
  7.2 87.0 %all-gather.4.cloned.1.call-start = ((), (), s32[]{:S(2)}) async-start(), calls=%async_computation.4 | async-start | bytes 4325376 | tf_op jit(solution)/shard_map/all_gather | solution.py:81
  7.9 126.3 %reduce-scatter.3.cloned.1.call-start = ((), (), s32[]{:S(2)}) async-start(), calls=%async_computation.5 | async-start | bytes 1179648 | tf_op jit(solution)/shard_map/reduce_scatter | solution.py:84
  11.9 86.4 %copy-start.5 = (s32[8,2]{0,1:T(2,128)S(1)}, s32[8,2]{0,1:T(2,128)}, u32[]{:S(2)}) copy-start(s32[8,2]{0,1:T(2,128)} %param.25) | copy-start | bytes 196
  11.9 122.3 %copy-start.1 = (bf16[8,4096]{1,0:T(8,128)(2,1)S(1)}, bf16[8,4096]{1,0:T(8,128)(2,1)}, u32[]{:S(2)}) copy-start(bf16[8,4096]{1,0:T(8,128)(2,1)} %param.16) | copy-start | bytes 196612
  11.9 123.4 %copy-start.2 = (f32[4096]{0:T(1024)S(1)}, f32[4096]{0:T(1024)}, u32[]{:S(2)}) copy-start(f32[4096]{0:T(1024)} %param.23) | copy-start | bytes 49156
  94.2 59.9 %copy-start.9 = (bf16[4096,8]{0,1:T(8,128)(2,1)S(1)}, bf16[4096,8]{0,1:T(8,128)(2,1)}, u32[]{:S(2)}) copy-start(bf16[4096,8]{0,1:T(8,128)(2,1)} %param.24) | copy-start | bytes 196612
  98.9 38.3 %all-to-all-start = ((s32[8,1,8]{2,1,0:T(1,128)}), s32[8,1,8]{2,1,0:T(1,128)S(1)}, u32[]{:S(2)}, u32[]{:S(2)}) async-start(s32[8,1,8]{2,1,0:T(1,128)} %compare_select_fusion.1), calls=%async_computation | async-start | bytes 8192 | tf_op jit(solution)/shard_map/all_to_all | solution.py:97
  137.2 15.7 %all-to-all-start.1 = ((bf16[8,8,4096]{2,1,0:T(8,128)(2,1)}), bf16[8,8,4096]{2,1,0:T(8,128)(2,1)S(1)}, u32[]{:S(2)}, u32[]{:S(2)}) async-start(bf16[8,8,4096]{2,1,0:T(8,128)(2,1)} %broadcast_select_fusion), calls=%async_computation.2 | async-start | bytes 1048576 | tf_op jit(solution)/shard_map/all_to_all | solution.py:96
  143.5 97.8 %all-gather.6.cloned.1.call-start = ((), (), s32[]{:S(2)}) async-start(), calls=%async_computation.6 | async-start | bytes 6488064 | tf_op jit(solution)/shard_map/all_gather | solution.py:125
  153.8 134.2 %reduce-scatter.5.cloned.1.call-start = ((), (), s32[]{:S(2)}) async-start(), calls=%async_computation.7 | async-start | bytes 1179648 | tf_op jit(solution)/shard_map/reduce_scatter | solution.py:144
  241.3 7.1 %copy-start.6 = (bf16[768,1,4096]{2,0,1:T(8,128)(2,1)S(1)}, bf16[768,1,4096]{2,0,1:T(8,128)(2,1)}, u32[]{:S(2)}) copy-start(bf16[768,1,4096]{2,0,1:T(8,128)(2,1)} %all-gather.6.cloned.1.call-done) | copy-start | bytes 18874372
  241.3 7.1 %copy-start.7 = (bf16[1,4096,448]{1,2,0:T(8,128)(2,1)S(1)}, bf16[1,4096,448]{1,2,0:T(8,128)(2,1)}, u32[]{:S(2)}) copy-start(bf16[1,4096,448]{1,2,0:T(8,128)(2,1)} %param.27) | copy-start | bytes 11010052
  251.8 5.8 %copy-start.10 = (s32[64]{0:T(128)S(1)}, s32[64]{0:T(128)}, u32[]{:S(2)}) copy-start(s32[64]{0:T(128)} %param.31) | copy-start | bytes 772
  251.8 36.3 %copy-start.11 = (f32[4]{0:T(128)S(1)}, f32[4]{0:T(128)}, u32[]{:S(2)}) copy-start(f32[4]{0:T(128)} %param.30) | copy-start | bytes 52
  251.8 196.8 %copy-start.3 = (f32[512]{0:T(512)S(1)}, f32[512]{0:T(512)}, u32[]{:S(2)}) copy-start(f32[512]{0:T(512)} %param.29) | copy-start | bytes 6148
  257.5 173.3 %all-reduce.2.cloned.1.call-start = ((), (), s32[]{:S(2)}) async-start(), calls=%async_computation.8 | async-start | bytes 262144 | tf_op jit(solution)/shard_map/psum | solution.py:145
  449.6 3.0 copy-start.4
Sparse Core Ops, SparseCore 0:
  10.5 83.7 all-gather.3
  98.4 35.7 reduce-scatter.2
  153.9 87.3 all-gather.5
  257.7 30.3 reduce-scatter.4
  291.3 139.4 all-reduce.1
where the time goes:
time: 460 us; the launch traced here: 459 us
  waiting for transfers between devices  341 us (74%)
  blocking collectives  53 us (12%)
  matrix products  27.4 us (6%)
  starting transfers between devices  14.2 us (3%)
  between operations  14.1 us (3%)
  other arithmetic  7.17 us (2%)
    psum x1, waiting for transfers between devices, shards(): pooled_cols = lax.psum(pooled_cols, 'dp')  143 us
    all_gather x1, waiting for transfers between devices, shards(): lax.all_gather(out_weight, 'dp', axis=1, tiled=True)  82.2 us
    all_gather x1, waiting for transfers between devices, shards(): gathered = lax.all_gather(compact, 'dp', axis=0, tiled=True)  49.7 us
    all_gather x1, blocking collectives, shards(): gathered_weight = lax.all_gather(pool_weight, 'dp', axis=0, tiled=True)  36.3 us
    reduce_scatter x1, waiting for transfers between devices, shards(): lax.psum_scatter(pooled_part, 'expert', scatter_dimension=1, tiled=True)  30.3 us
    reduce_scatter x1, waiting for transfers between devices, shards(): lax.psum_scatter(head_terms, 'expert', scatter_dimension=0, tiled=True)  27.6 us
    psum x1, blocking collectives, shards(): squares = lax.psum(jnp.sum(pooled_cols * pooled_cols, axis=-1), 'expert')  16.7 us
  transfers between devices with their start and end apart: 7, of which 6 were waited for; matrix products, arithmetic and copies ran while one was open for 2% of the time, Pallas kernels for 0%

commit v1 on v0

--- a/solution.py
+++ b/solution.py
@@ -142,7 +142,11 @@
         (jnp.arange(span_count) == own_span)[:, None], mixed_sum[None, :], 0.0
     )
     pooled_cols = lax.psum_scatter(pooled_part, "expert", scatter_dimension=1, tiled=True)
-    pooled_cols = lax.psum(pooled_cols, "dp")
+    pooled_cols = pooled_cols
+    for hop in (1, 2, 4, 8, 16):
+        pooled_cols = pooled_cols + lax.ppermute(
+            pooled_cols, "dp", [(dev, dev ^ hop) for dev in range(32)]
+        )
     squares = lax.psum(jnp.sum(pooled_cols * pooled_cols, axis=-1), "expert")
     everyone = (pooled_cols * lax.rsqrt(squares / width + EPSILON)[:, None] * summary_gain).astype(
         jnp.bfloat16

time: 460 us -> 350 us (0.76)
  waiting for transfers between devices: 341 us -> 214 us
  starting transfers between devices: 14.2 us -> 26.7 us
  blocking collectives: 53 us -> 59.9 us
    psum x1 -> x0, waiting for transfers between devices: 143 us -> none  [shards(): pooled_cols = lax.psum(pooled_cols, 'dp')]
    ppermute x0 -> x5, waiting for transfers between devices: none -> 15.7 us  [shards(): lax.ppermute(pooled_cols, 'dp', [(dev, dev ^ hop) for dev in range(32)])]
    ppermute x0 -> x5, starting transfers between devices: none -> 12.6 us  [shards(): lax.ppermute(pooled_cols, 'dp', [(dev, dev ^ hop) for dev in range(32)])]
    psum x1, blocking collectives: 16.7 us -> 23.6 us  [shards(): squares = lax.psum(jnp.sum(pooled_cols * pooled_cols, axis=-1), 'expert')]
  transfers between devices with their start and end apart: 7 -> 11, of which waited for: 6 -> 10; matrix products, arithmetic and copies ran while one was open for 2% -> 3% of each run, Pallas kernels for 0% -> 0%
where the time goes in v1:
time: 350 us; the launch traced here: 349 us
  waiting for transfers between devices  214 us (61%)
  blocking collectives  59.9 us (17%)
  starting transfers between devices  26.7 us (8%)
  matrix products  25.6 us (7%)
  between operations  14.1 us (4%)
  other arithmetic  6.35 us (2%)
    all_gather x1, waiting for transfers between devices, shards(): lax.all_gather(out_weight, 'dp', axis=1, tiled=True)  82.2 us
    all_gather x1, waiting for transfers between devices, shards(): gathered = lax.all_gather(compact, 'dp', axis=0, tiled=True)  49.7 us
    all_gather x1, blocking collectives, shards(): gathered_weight = lax.all_gather(pool_weight, 'dp', axis=0, tiled=True)  36.3 us
    reduce_scatter x1, waiting for transfers between devices, shards(): lax.psum_scatter(pooled_part, 'expert', scatter_dimension=1, tiled=True)  30.5 us
    reduce_scatter x1, waiting for transfers between devices, shards(): lax.psum_scatter(head_terms, 'expert', scatter_dimension=0, tiled=True)  27.6 us
    psum x1, blocking collectives, shards(): squares = lax.psum(jnp.sum(pooled_cols * pooled_cols, axis=-1), 'expert')  23.6 us
    ppermute x5, waiting for transfers between devices, shards(): lax.ppermute(pooled_cols, 'dp', [(dev, dev ^ hop) for dev in range(32)])  15.7 us
    ppermute x5, starting transfers between devices, shards(): lax.ppermute(pooled_cols, 'dp', [(dev, dev ^ hop) for dev in range(32)])  12.6 us
  transfers between devices with their start and end apart: 11, of which 10 were waited for; matrix products, arithmetic and copies ran while one was open for 3% of the time, Pallas kernels for 0%

profile of v1, /device:TPU:1, one launch (start us, length us, event | category | flops | bytes accessed | tf_op | source)
XLA Modules:
  0.0 349.0 jit_solution(8707688940483696549)
XLA Ops:
  7.2 0.0 copy-start
  7.2 0.0 all-gather.4.cloned.1.call-start
  7.2 0.7 all-gather.4.cloned.1.call-update
  7.9 0.0 reduce-scatter.3.cloned.1.call-start
  8.0 0.9 reshape.501
  8.9 0.4 fusion.59
  9.2 1.0 fusion.60
  10.3 0.3 fusion.27
  10.6 0.9 fusion.40
  11.5 0.4 fusion.22
  11.9 0.0 copy-start.5
  11.9 0.0 copy-start.1
  12.0 82.2 %all-gather.4.cloned.1.call-done = bf16[512,4096]{1,0:T(8,128)(2,1)} async-done(((bf16[512,128]{1,0:T(8,128)(2,1)}), bf16[512,4096]{1,0:T(8,128)(2,1)}) %all-gather.4.cloned.1.call-update) | async-done | bytes 4194320 | tf_op jit(solution)/shard_map/all_gather | solution.py:81
  94.2 4.0 %fusion.35 = f32[64,4096]{1,0:T(8,128)} fusion(bf16[512,4096]{1,0:T(8,128)(2,1)} %all-gather.4.cloned.1.call-done, bf16[8,8,4,128]{3,2,1,0:T(4,128)(2,1)S(1)} %bitcast.123), kind=kOutput, calls=%fused_computation.44 | convolution fusion | flops 268435456 | bytes 5308416 | tf_op jit(solution)/shard_map/dot_general | solution.py:79
  98.3 0.0 reduce-scatter.3.cloned.1.call-update
  98.3 0.6 compare_select_fusion.1
  98.9 7.7 %all-to-all-start = ((s32[8,1,8]{2,1,0:T(1,128)}), s32[8,1,8]{2,1,0:T(1,128)S(1)}, u32[]{:S(2)}, u32[]{:S(2)}) async-start(s32[8,1,8]{2,1,0:T(1,128)} %compare_select_fusion.1), calls=%async_computation | async-start | bytes 8192 | tf_op jit(solution)/shard_map/all_to_all | solution.py:97
  106.6 27.6 %reduce-scatter.3.cloned.1.call-done = f32[8,4096]{1,0:T(8,128)} async-done(((f32[64,4096]{1,0:T(8,128)}), f32[8,4096]{1,0:T(8,128)}) %reduce-scatter.3.cloned.1.call-update) | async-done | bytes 131088 | tf_op jit(solution)/shard_map/reduce_scatter | solution.py:84
  134.2 1.1 fusion.47
  135.3 1.0 multiply_convert_fusion.1
  136.3 0.9 broadcast_select_fusion
  137.2 6.3 %all-to-all-start.1 = ((bf16[8,8,4096]{2,1,0:T(8,128)(2,1)}), bf16[8,8,4096]{2,1,0:T(8,128)(2,1)S(1)}, u32[]{:S(2)}, u32[]{:S(2)}) async-start(bf16[8,8,4096]{2,1,0:T(8,128)(2,1)} %broadcast_select_fusion), calls=%async_computation.2 | async-start | bytes 1048576 | tf_op jit(solution)/shard_map/all_to_all | solution.py:96
  143.5 0.5 broadcast.319
  144.0 0.7 fusion.58
  144.7 0.1 reshape.524
  144.8 0.1 reduce-window.7
  144.9 0.1 all_to_all.8
  145.0 0.1 add_reduce_fusion
  145.1 7.8 %all-to-all-done.1 = bf16[8,8,4096]{2,1,0:T(8,128)(2,1)S(1)} async-done(((bf16[8,8,4096]{2,1,0:T(8,128)(2,1)}), bf16[8,8,4096]{2,1,0:T(8,128)(2,1)S(1)}, u32[]{:S(2)}, u32[]{:S(2)}) %all-to-all-start.1) | async-done | bytes 524320 | tf_op jit(solution)/shard_map/all_to_all | solution.py:96
  152.9 0.9 convolution_convert_fusion
  153.8 0.0 all-gather.6.cloned.1.call-update
  153.8 0.0 reduce-scatter.5.cloned.1.call-start
  153.9 0.1 fusion.50
  154.0 0.1 select_reduce_fusion.1
  154.2 1.1 select_reduce_fusion.2
  155.3 36.3 %all-gather = f32[32,24,2]{1,2,0:T(2,128)S(1)} all-gather(f32[1,24,2]{1,2,0:T(2,128)S(1)} %fusion.56), channel_id=1, replica_groups=mesh['dp'=32,'expert'=8] {'dp'}, dimensions={0}, use_global_device_ids=true | all-gather | bytes 6336 | tf_op jit(solution)/shard_map/all_gather | solution.py:126
  191.6 49.7 %all-gather.6.cloned.1.call-done = bf16[768,1,4096]{2,0,1:T(8,128)(2,1)} async-done(((bf16[24,1,4096]{2,0,1:T(8,128)(2,1)}), bf16[768,1,4096]{2,0,1:T(8,128)(2,1)}) %all-gather.6.cloned.1.call-update) | async-done | bytes 6291472 | tf_op jit(solution)/shard_map/all_gather | solution.py:125
  241.3 7.0 %fusion.3 = f32[768,448]{0,1:T(8,128)S(1)} fusion(bf16[768,1,4096]{2,0,1:T(8,128)(2,1)} %all-gather.6.cloned.1.call-done, bf16[1,4096,448]{1,2,0:T(8,128)(2,1)} %param.26), kind=kOutput, calls=%fused_computation.3 | convolution fusion | flops 2818572288 | bytes 11337728 | tf_op jit(solution)/shard_map/ned,edf->nf/dot_general | solution.py:128
  248.4 3.1 fusion.14
  251.5 0.3 copy.46
  251.8 0.5 fusion.66
  252.3 0.1 reshape.513
  252.4 5.1 %convolution_add_fusion = f32[64,4096]{1,0:T(8,128)} fusion(f32[64,448]{1,0:T(8,128)S(1)} %reshape.513, bf16[1,448,4096]{2,1,0:T(8,128)(2,1)} %param.28, f32[4096]{0:T(1024)S(1)} %get-tuple-element.2, pred[64]{0:T(512)(128)(4,1)S(1)} %iota_compare_fusion.5), kind=kOutput, calls=%fused_computation.5 | convolution fusion | flops 1409810432 | bytes 4849728 | tf_op jit(solution)/shard_map/dot_general | solution.py:137
  257.5 0.0 reduce-scatter.5.cloned.1.call-update
  257.5 30.5 %reduce-scatter.5.cloned.1.call-done = f32[64,512]{1,0:T(8,128)} async-done(((f32[64,4096]{1,0:T(8,128)}), f32[64,512]{1,0:T(8,128)}) %reduce-scatter.5.cloned.1.call-update) | async-done | bytes 131088 | tf_op jit(solution)/shard_map/reduce_scatter | solution.py:144
  288.0 0.9 collective-permute-start
  288.9 3.2 collective-permute-done
  292.1 0.9 add.95
  293.0 2.5 collective-permute-start.1
  295.5 3.5 collective-permute-done.1
  299.0 1.4 collective-permute-start.2
  300.4 0.1 dynamic_slice.7
  300.4 2.8 collective-permute-done.2
  303.2 2.3 collective-permute-start.3
  305.5 0.1 broadcast_compare_fusion
  305.6 3.8 %collective-permute-done.3 = f32[64,512]{1,0:T(8,128)S(1)} collective-permute-done((f32[64,512]{1,0:T(8,128)S(1)}, f32[64,512]{1,0:T(8,128)S(1)}, u32[]{:S(2)}, u32[]{:S(2)}) %collective-permute-start.3) | collective-permute-done | bytes 131104 | tf_op jit(solution)/shard_map/ppermute | solution.py:147
  309.4 5.5 %collective-permute-start.4 = (f32[64,512]{1,0:T(8,128)S(1)}, f32[64,512]{1,0:T(8,128)S(1)}, u32[]{:S(2)}, u32[]{:S(2)}) collective-permute-start(f32[64,512]{1,0:T(8,128)S(1)} %add.98), channel_id=1, source_target_pairs={{0,128},{8,136},{16,144},{24,152},{32,160},{40,168},{48,176},{56,1... | collective-permute-start | bytes 393224 | tf_op jit(solution)/shard_map/ppermute | solution.py:147
  315.0 2.5 collective-permute-done.4
  317.5 0.1 multiply_reduce_fusion
  317.6 23.6 %psum.7 = f32[64]{0:T(128)S(1)} all-reduce(f32[64]{0:T(128)S(1)} %get-tuple-element.10), channel_id=1, replica_groups=mesh['dp'=32,'expert'=8] {'expert'}, use_global_device_ids=true, to_apply=%region_15.16 | all-reduce | flops 64 | bytes 512 | tf_op jit(solution)/shard_map/psum | solution.py:150
  341.2 0.1 multiply_convert_fusion
  341.3 0.0 copy-start.4
  341.3 0.4 fusion.61
  341.7 0.8 fusion.26
  (42 shorter events, 0.3 us)
Async XLA Ops:
  7.2 1.7 copy-start
  7.2 4.3 %copy-start.8 = (bf16[2,1024,128]{2,1,0:T(8,128)(2,1)S(1)}, bf16[2,1024,128]{2,1,0:T(8,128)(2,1)}, u32[]{:S(2)}) copy-start(bf16[2,1024,128]{2,1,0:T(8,128)(2,1)} %param.21) | copy-start | bytes 1572868
  7.2 87.0 %all-gather.4.cloned.1.call-start = ((), (), s32[]{:S(2)}) async-start(), calls=%async_computation.4 | async-start | bytes 4325376 | tf_op jit(solution)/shard_map/all_gather | solution.py:81
  7.9 126.3 %reduce-scatter.3.cloned.1.call-start = ((), (), s32[]{:S(2)}) async-start(), calls=%async_computation.5 | async-start | bytes 1179648 | tf_op jit(solution)/shard_map/reduce_scatter | solution.py:84
  11.9 86.4 %copy-start.5 = (s32[8,2]{0,1:T(2,128)S(1)}, s32[8,2]{0,1:T(2,128)}, u32[]{:S(2)}) copy-start(s32[8,2]{0,1:T(2,128)} %param.25) | copy-start | bytes 196
  11.9 122.3 %copy-start.1 = (bf16[8,4096]{1,0:T(8,128)(2,1)S(1)}, bf16[8,4096]{1,0:T(8,128)(2,1)}, u32[]{:S(2)}) copy-start(bf16[8,4096]{1,0:T(8,128)(2,1)} %param.16) | copy-start | bytes 196612
  11.9 123.4 %copy-start.2 = (f32[4096]{0:T(1024)S(1)}, f32[4096]{0:T(1024)}, u32[]{:S(2)}) copy-start(f32[4096]{0:T(1024)} %param.23) | copy-start | bytes 49156
  94.2 59.9 %copy-start.9 = (bf16[4096,8]{0,1:T(8,128)(2,1)S(1)}, bf16[4096,8]{0,1:T(8,128)(2,1)}, u32[]{:S(2)}) copy-start(bf16[4096,8]{0,1:T(8,128)(2,1)} %param.24) | copy-start | bytes 196612
  98.9 38.3 %all-to-all-start = ((s32[8,1,8]{2,1,0:T(1,128)}), s32[8,1,8]{2,1,0:T(1,128)S(1)}, u32[]{:S(2)}, u32[]{:S(2)}) async-start(s32[8,1,8]{2,1,0:T(1,128)} %compare_select_fusion.1), calls=%async_computation | async-start | bytes 8192 | tf_op jit(solution)/shard_map/all_to_all | solution.py:97
  137.2 15.7 %all-to-all-start.1 = ((bf16[8,8,4096]{2,1,0:T(8,128)(2,1)}), bf16[8,8,4096]{2,1,0:T(8,128)(2,1)S(1)}, u32[]{:S(2)}, u32[]{:S(2)}) async-start(bf16[8,8,4096]{2,1,0:T(8,128)(2,1)} %broadcast_select_fusion), calls=%async_computation.2 | async-start | bytes 1048576 | tf_op jit(solution)/shard_map/all_to_all | solution.py:96
  143.5 97.8 %all-gather.6.cloned.1.call-start = ((), (), s32[]{:S(2)}) async-start(), calls=%async_computation.6 | async-start | bytes 6488064 | tf_op jit(solution)/shard_map/all_gather | solution.py:125
  153.8 134.2 %reduce-scatter.5.cloned.1.call-start = ((), (), s32[]{:S(2)}) async-start(), calls=%async_computation.7 | async-start | bytes 1179648 | tf_op jit(solution)/shard_map/reduce_scatter | solution.py:144
  241.3 7.1 %copy-start.6 = (bf16[768,1,4096]{2,0,1:T(8,128)(2,1)S(1)}, bf16[768,1,4096]{2,0,1:T(8,128)(2,1)}, u32[]{:S(2)}) copy-start(bf16[768,1,4096]{2,0,1:T(8,128)(2,1)} %all-gather.6.cloned.1.call-done) | copy-start | bytes 18874372
  241.3 7.1 %copy-start.7 = (bf16[1,4096,448]{1,2,0:T(8,128)(2,1)S(1)}, bf16[1,4096,448]{1,2,0:T(8,128)(2,1)}, u32[]{:S(2)}) copy-start(bf16[1,4096,448]{1,2,0:T(8,128)(2,1)} %param.27) | copy-start | bytes 11010052
  252.3 48.0 %copy-start.10 = (s32[64]{0:T(128)S(1)}, s32[64]{0:T(128)}, u32[]{:S(2)}) copy-start(s32[64]{0:T(128)} %param.31) | copy-start | bytes 772
  252.4 62.5 %copy-start.11 = (f32[4]{0:T(128)S(1)}, f32[4]{0:T(128)}, u32[]{:S(2)}) copy-start(f32[4]{0:T(128)} %param.30) | copy-start | bytes 52
  252.4 88.8 %copy-start.3 = (f32[512]{0:T(512)S(1)}, f32[512]{0:T(512)}, u32[]{:S(2)}) copy-start(f32[512]{0:T(512)} %param.29) | copy-start | bytes 6148
  288.0 4.0 %collective-permute-start = (f32[64,512]{1,0:T(8,128)}, f32[64,512]{1,0:T(8,128)S(1)}, u32[]{:S(2)}, u32[]{:S(2)}) collective-permute-start(f32[64,512]{1,0:T(8,128)} %reduce-scatter.5.cloned.1.call-done), channel_id=1, source_target_pairs={{0,8},{8,0},{16,24},{24,16},{32,40},{40,32},{48,56},{56,48},{64,72... | collective-permute-start | bytes 393224 | tf_op jit(solution)/shard_map/ppermute | solution.py:147
  293.0 6.0 %collective-permute-start.1 = (f32[64,512]{1,0:T(8,128)S(1)}, f32[64,512]{1,0:T(8,128)S(1)}, u32[]{:S(2)}, u32[]{:S(2)}) collective-permute-start(f32[64,512]{1,0:T(8,128)S(1)} %add.95), channel_id=1, source_target_pairs={{0,16},{8,24},{16,0},{24,8},{32,48},{40,56},{48,32},{56,40},{64,80... | collective-permute-start | bytes 393224 | tf_op jit(solution)/shard_map/ppermute | solution.py:147
  299.0 4.2 %collective-permute-start.2 = (f32[64,512]{1,0:T(8,128)S(1)}, f32[64,512]{1,0:T(8,128)S(1)}, u32[]{:S(2)}, u32[]{:S(2)}) collective-permute-start(f32[64,512]{1,0:T(8,128)S(1)} %add.96), channel_id=1, source_target_pairs={{0,32},{8,40},{16,48},{24,56},{32,0},{40,8},{48,16},{56,24},{64,96... | collective-permute-start | bytes 393224 | tf_op jit(solution)/shard_map/ppermute | solution.py:147
  303.2 6.2 %collective-permute-start.3 = (f32[64,512]{1,0:T(8,128)S(1)}, f32[64,512]{1,0:T(8,128)S(1)}, u32[]{:S(2)}, u32[]{:S(2)}) collective-permute-start(f32[64,512]{1,0:T(8,128)S(1)} %add.97), channel_id=1, source_target_pairs={{0,64},{8,72},{16,80},{24,88},{32,96},{40,104},{48,112},{56,120},{... | collective-permute-start | bytes 393224 | tf_op jit(solution)/shard_map/ppermute | solution.py:147
  309.4 8.1 %collective-permute-start.4 = (f32[64,512]{1,0:T(8,128)S(1)}, f32[64,512]{1,0:T(8,128)S(1)}, u32[]{:S(2)}, u32[]{:S(2)}) collective-permute-start(f32[64,512]{1,0:T(8,128)S(1)} %add.98), channel_id=1, source_target_pairs={{0,128},{8,136},{16,144},{24,152},{32,160},{40,168},{48,176},{56,1... | collective-permute-start | bytes 393224 | tf_op jit(solution)/shard_map/ppermute | solution.py:147
  341.3 1.2 copy-start.4
Sparse Core Ops, SparseCore 0:
  10.5 83.7 all-gather.3
  98.4 35.7 reduce-scatter.2
  153.9 87.3 all-gather.5
  257.7 30.3 reduce-scatter.4
